TPU v7x, 256 devices: a whole 4x4x8 slice. The times are simulated.
256 devices in a mesh: rep: 16 (over z, core), wide: 4 (over x), narrow: 4 (over y).
Axes of the slice: x: 4, y: 4, z: 8, core: 2. Of those that a mesh axis runs over, the one named last changes fastest.
Arguments:
- tokens: bfloat16 [16384, 1536], P(('rep', 'wide'), 'narrow'), parts along dimension 0, may hold values from -6 to 6
- attn_gain: float32 [1536], replicated, may hold values from 0.1 to 1.9
- w_qkv: bfloat16 [1536, 2048], P(None, ('wide', 'narrow')), may hold values from -0.15625 to 0.15625
- w_out: bfloat16 [1536, 1536], P(None, 'narrow'), may hold values from -0.15625 to 0.15625
- prefix_cache: bfloat16 [2, 32, 8192, 2, 128], P(None, 'rep', ('wide', 'narrow')), parts along dimension 1, may hold values from -1500 to 1500
- decode_cache: bfloat16 [2, 64, 8192, 2, 128], P(None, 'rep', ('wide', 'narrow')), parts along dimension 1, may hold values from -1500 to 1500
- offsets: int32 [32], P('rep'), parts along dimension 0, may hold values from 1 to 8192, as said below
- lengths: int32 [64], P('rep'), parts along dimension 0, may hold values from 1 to 8192, as said below
Outputs:
- mixed: bfloat16 [16384, 1536], P(('rep', 'wide'), 'narrow'), parts along dimension 0
There are 16 independent parts, one for each index of `rep`. A program takes and returns all parts, laid end to end along the dimension named above; an argument that names none is the same for every part. Nothing has to cross between parts.
Inputs may be any that keep to these rules, and one draw needn't show every extreme that they name: `offsets`: exactly one prefill block has 8192 cached positions. `lengths`: exactly one decode has 8192 cached positions.
All inputs are finite; a program needn't handle non-finite values.
Results may differ from a plain program's by a relative error of at most 0.008.
Values may be sent and summed in bfloat16 or wider, within the bound.
No kernel may reach another device: no remote copies, remote signals or barrier semaphores. Data moves between devices by JAX's collectives and lax.ppermute only.
A program may use at most 320 MiB of HBM per device.

v0:
```python
import jax
import jax.numpy as jnp
from jax import lax
from jax.sharding import PartitionSpec as P

EPS = 1e-06
NEG = -1e30


def normalize(rows, gain):
    full = rows.astype(jnp.float32)
    meansq = jnp.mean(full * full, -1, keepdims=True)
    return (full * lax.rsqrt(meansq + EPS) * gain).astype(jnp.bfloat16)


def partial_softmax(grouped_queries, keys, values, allowed, form_s, form_o):
    scores = jnp.einsum(
        form_s, grouped_queries, keys, preferred_element_type=jnp.float32
    ) * grouped_queries.shape[-1] ** (-0.5)
    masked = jnp.where(allowed, scores, NEG)
    peak = jnp.max(masked, -1)
    weights = jnp.where(allowed, jnp.exp(masked - peak[..., None]), 0.0)
    total = jnp.sum(weights, -1)
    weighted = jnp.einsum(
        form_o, weights.astype(jnp.bfloat16), values, preferred_element_type=jnp.float32
    )
    return (peak, total, weighted)


def join_parts(first, second):
    peak = jnp.maximum(first[0], second[0])
    scale_a = jnp.exp(first[0] - peak)
    scale_b = jnp.exp(second[0] - peak)
    total = first[1] * scale_a + second[1] * scale_b
    weighted = first[2] * heads_major(scale_a) + second[2] * heads_major(scale_b)
    return (peak, total, weighted)


def heads_major(scale):
    return scale.transpose(1, 2, 0)[..., None]


def per_device(tokens, attn_gain, w_qkv, w_out, prefix_cache, decode_cache, offsets, lengths):
    n_wide = lax.axis_size("wide")
    n_narrow = lax.axis_size("narrow")
    devices = n_wide * n_narrow
    joined = lax.axis_index("wide") * n_narrow + lax.axis_index("narrow")
    block_rows = tokens.shape[0]
    every_rows = block_rows * n_wide
    own = every_rows // devices
    head_dim = prefix_cache.shape[-1]
    kv_heads = prefix_cache.shape[-2]
    n_prefix = prefix_cache.shape[1]
    n_decode = decode_cache.shape[1]
    span = (every_rows - n_decode) // n_prefix
    q_width = w_out.shape[0]
    heads = q_width // head_dim
    group = heads // kv_heads
    starts = (offsets[:, None] + jnp.arange(span, dtype=jnp.int32)[None, :]).reshape(-1)
    positions = jnp.concatenate([starts, lengths])
    row_ids = jnp.arange(every_rows, dtype=jnp.int32)
    sequence = jnp.where(
        row_ids < n_prefix * span, row_ids // span, row_ids - n_prefix * span + n_prefix
    )
    own_start = joined * own
    own_pos = lax.dynamic_slice_in_dim(positions, own_start, own)
    own_seq = lax.dynamic_slice_in_dim(sequence, own_start, own)
    features = lax.all_gather(tokens, "narrow", axis=1, tiled=True)
    normed_rows = normalize(features, attn_gain)
    w_cols = lax.all_gather(w_qkv, "wide", axis=0, tiled=False)
    part = jnp.einsum(
        "rf,wfc->rwc", normed_rows, w_cols, preferred_element_type=jnp.float32
    ).astype(jnp.bfloat16)
    col_block = w_qkv.shape[1]
    q_blocks = q_width // (n_narrow * col_block)
    gathered = lax.all_gather(part[:, :q_blocks], ("wide", "narrow"), axis=0, tiled=False)
    query_matrix = (
        gathered.reshape(n_wide, n_narrow, block_rows, q_blocks, col_block)
        .transpose(0, 2, 3, 1, 4)
        .reshape(every_rows, heads, head_dim)
    )
    fresh_kv = part[:, q_blocks:].reshape(n_narrow, own, col_block)
    fresh_kv = lax.all_to_all(fresh_kv, "narrow", 0, 0)
    own_keys = fresh_kv[:kv_heads].transpose(1, 0, 2)
    own_values = fresh_kv[kv_heads:].transpose(1, 0, 2)
    grouped_queries = query_matrix.reshape(every_rows, kv_heads, group, head_dim)
    shard = prefix_cache.shape[2]
    cache_pos = joined * shard + jnp.arange(shard, dtype=jnp.int32)
    pieces = []
    for index in range(n_prefix):
        block = grouped_queries[index * span : (index + 1) * span]
        allowed = (cache_pos < offsets[index])[None, None, None, :]
        pieces.append(
            partial_softmax(
                block,
                prefix_cache[0, index],
                prefix_cache[1, index],
                allowed,
                "qhgd,khd->qhgk",
                "qhgk,khd->hgqd",
            )
        )
    allowed = (cache_pos[None, :] < lengths[:, None])[:, None, None, :]
    pieces.append(
        partial_softmax(
            grouped_queries[n_prefix * span :],
            decode_cache[0],
            decode_cache[1],
            allowed,
            "nhgd,nkhd->nhgk",
            "nhgk,nkhd->hgnd",
        )
    )
    cached = tuple(
        (jnp.concatenate([piece[slot] for piece in pieces], 2 * (slot // 2)) for slot in range(3))
    )
    allowed = ((sequence[:, None] == own_seq[None, :]) & (own_pos[None, :] <= positions[:, None]))[
        :, None, None, :
    ]
    fresh = partial_softmax(
        grouped_queries, own_keys, own_values, allowed, "rhgd,khd->rhgk", "rhgk,khd->hgrd"
    )
    peak, total, weighted = join_parts(cached, fresh)
    top = lax.pmax(peak, "narrow")
    hi = lax.reduce_precision(top, exponent_bits=8, mantissa_bits=7)
    lo = lax.reduce_precision(top - hi, exponent_bits=8, mantissa_bits=7)
    shift = hi + lo
    scale = jnp.exp(jnp.minimum(peak - shift, 80.0))
    first = lax.axis_index("narrow") == 0

    def kept(a):
        return jnp.where(first, a, jnp.zeros_like(a)).reshape(every_rows, heads)

    lanes = 128
    extra = jnp.concatenate(
        [
            (total * scale).reshape(every_rows, heads),
            kept(hi),
            kept(lo),
            jnp.zeros((every_rows, lanes - 3 * heads), jnp.float32),
        ],
        1,
    )
    scaled = (weighted * heads_major(scale)).reshape(heads, every_rows, head_dim)
    packed = jnp.concatenate([scaled, extra[None]], 0).astype(jnp.bfloat16)
    slots = packed.shape[0]
    packed = (
        packed.reshape(slots, n_wide, n_narrow, own, head_dim)
        .transpose(0, 2, 1, 3, 4)
        .reshape(slots, every_rows, head_dim)
    )
    packed = lax.psum_scatter(packed, "narrow", scatter_dimension=1, tiled=True)
    packed = lax.all_to_all(packed.reshape(slots, n_wide, own, head_dim), "wide", 1, 1)
    packed = packed.astype(jnp.float32)
    extra = packed[heads]
    part_shift = extra[..., heads : 2 * heads] + extra[..., 2 * heads : 3 * heads]
    part_scale = jnp.exp(part_shift - jnp.max(part_shift, 0)[None])
    total = jnp.sum(extra[..., :heads] * part_scale, 0)
    weighted = jnp.sum(packed[:heads] * part_scale.transpose(2, 0, 1)[..., None], 1)
    attended = weighted / total.T[..., None]
    attended = attended.astype(jnp.bfloat16).transpose(1, 0, 2).reshape(own, q_width)
    mine_rows = lax.all_gather(attended, "narrow", axis=0, tiled=True)
    mixed = tokens.astype(jnp.float32) + jnp.dot(
        mine_rows, w_out, preferred_element_type=jnp.float32
    )
    return mixed.astype(jnp.bfloat16)


def solution(mesh):
    return jax.shard_map(
        per_device,
        mesh=mesh,
        in_specs=(
            P(("rep", "wide"), "narrow"),
            P(),
            P(None, ("wide", "narrow")),
            P(None, "narrow"),
            P(None, "rep", ("wide", "narrow"), None, None),
            P(None, "rep", ("wide", "narrow"), None, None),
            P("rep"),
            P("rep"),
        ),
        out_specs=P(("rep", "wide"), "narrow"),
        check_vma=False,
    )
```

profile of v0, /device:TPU:32, one launch (start us, length us, event | category | flops | bytes accessed | tf_op | source)
XLA Modules:
  0.0 237.3 jit_solution(5814794510141817188)
XLA Ops:
  6.5 0.0 all-gather.5.cloned.1.call-start
  6.6 0.7 all-gather.5.cloned.1.call-update
  7.3 0.0 all-gather.7.cloned.1.call-start
  7.3 14.8 %all_gather.18 = bf16[256,1536]{1,0:T(8,128)(2,1)S(1)} all-gather(bf16[256,384]{1,0:T(8,128)(2,1)} %param.8), channel_id=1, replica_groups=mesh['rep'=16,'wide'=4,'narrow'=4] {'narrow'}, dimensions={1}, use_global_device_ids=true | all-gather | bytes 983040 | tf_op jit(solution)/shard_map/all_gather | solution.py:68
  22.1 0.2 fusion.28
  22.4 18.4 %all-gather.5.cloned.1.call-done = bf16[6144,128]{1,0:T(8,128)(2,1)} async-done(((bf16[1536,128]{1,0:T(8,128)(2,1)}), bf16[6144,128]{1,0:T(8,128)(2,1)}) %all-gather.5.cloned.1.call-update) | async-done | bytes 1572880 | tf_op jit(solution)/shard_map/all_gather | solution.py:70
  40.8 2.0 convolution_convert_fusion
  42.8 0.7 copy-done.7
  43.5 0.7 slice.80
  44.2 0.0 all-gather.7.cloned.1.call-update
  44.3 0.1 iota_add_fusion.1
  44.3 0.1 add.103
  44.4 0.1 fusion.71
  44.5 0.1 dynamic_slice.6
  44.6 0.1 dynamic_slice.7
  44.7 0.1 pad.4.clone
  44.7 0.7 fusion.93
  45.4 1.3 fusion.76
  46.7 0.1 broadcast_compare_fusion
  46.7 0.7 compare_and_fusion
  47.5 1.5 fusion.92
  49.0 1.5 fusion.91
  50.5 1.5 slice.84
  52.0 4.3 %all-to-all-start = ((bf16[4,64,128]{2,1,0:T(8,128)(2,1)}), bf16[4,64,128]{2,1,0:T(8,128)(2,1)}, u32[]{:S(2)}, u32[]{:S(2)}) async-start(bf16[4,64,128]{2,1,0:T(8,128)(2,1)} %bitcast.160), calls=%async_computation | async-start | bytes 131072 | tf_op jit(solution)/shard_map/all_to_all | solution.py:83
  56.3 41.0 %all-gather.7.cloned.1.call-done = bf16[4096,3,128]{2,0,1:T(8,128)(2,1)} async-done(((bf16[256,3,128]{2,0,1:T(8,128)(2,1)}), bf16[4096,3,128]{2,0,1:T(8,128)(2,1)}) %all-gather.7.cloned.1.call-update) | async-done | bytes 3145744 | tf_op jit(solution)/shard_map/all_gather | solution.py:76
  97.3 2.3 copy.85
  99.6 0.4 fusion.44
  100.0 0.2 fusion.88
  100.2 0.2 fusion.66
  100.4 1.9 bitcast_reduce_fusion
  102.3 3.6 %fusion.6 = f32[510,2,6]{0,2,1:T(8,128)S(1)} fusion(f32[2,510,6,512]{3,1,2,0:T(8,128)S(1)} %get-tuple-element.27, f32[510,2,6]{0,2,1:T(8,128)S(1)} %get-tuple-element.26, pred[512]{0:T(512)(128)(4,1)S(1)} %get-tuple-element.32), kind=kLoop, calls=%fused_computation.12 | loop fusion | flops 15661080 | bytes 12583232 | tf_op jit(solution)/shard_map/reduce_sum | solution.py:23
  105.9 4.2 %fusion.25 = f32[2,6,510,128]{3,2,1,0:T(8,128)} fusion(f32[2,510,6,512]{3,1,2,0:T(8,128)S(1)} %get-tuple-element.27, f32[510,2,6]{0,2,1:T(8,128)S(1)} %get-tuple-element.26, pred[512]{0:T(512)(128)(4,1)S(1)} %get-tuple-element.32, bf16[1,1,512,2,128]{4,3,2,1,0:T(2,128)(2,1)S(1)} %copy-done.9), kind=kOutput, calls=%fused_computation.34 | convolution fusion | flops 817827840 | bytes 15954336 | tf_op jit(solution)/shard_map/qhgk,khd->hgqd/dot_general | solution.py:24
  110.1 0.2 fusion.43
  110.4 0.0 all-to-all-done
  110.4 3.3 %fusion.19 = (f32[1024,2,6]{0,2,1:T(8,128)S(1)}, f32[2,64,1024,6]{2,1,3,0:T(8,128)S(1)}) fusion(pred[1024,64]{0,1:T(8,128)(4,1)S(1)} %copy-done.5, bf16[1024,2,6,128]{3,0,2,1:T(8,128)(2,1)} %bitcast.154, bf16[4,64,128]{2,1,0:T(8,128)(2,1)} %all-to-all-done), kind=kOutput, calls=%fused_computation.28 | convolution fusion | flops 203673600 | bytes 6438912 | tf_op jit(solution)/shard_map/rhgd,khd->rhgk/dot_general | solution.py:17
  113.7 0.8 fusion.20
  114.5 0.8 copy-done.3
  115.4 1.9 bitcast_reduce_fusion.1
  117.3 0.1 fusion.78
  117.4 3.6 %fusion.4 = f32[510,2,6]{0,2,1:T(8,128)S(1)} fusion(f32[2,510,6,512]{3,1,2,0:T(8,128)S(1)} %get-tuple-element.29, f32[510,2,6]{0,2,1:T(8,128)S(1)} %get-tuple-element.28, pred[512]{0:T(512)(128)(4,1)S(1)} %get-tuple-element.33), kind=kLoop, calls=%fused_computation.10 | loop fusion | flops 15661080 | bytes 12583232 | tf_op jit(solution)/shard_map/reduce_sum | solution.py:23
  121.0 4.2 %fusion.22 = f32[2,6,510,128]{3,2,1,0:T(8,128)} fusion(f32[2,510,6,512]{3,1,2,0:T(8,128)S(1)} %get-tuple-element.29, f32[510,2,6]{0,2,1:T(8,128)S(1)} %get-tuple-element.28, pred[512]{0:T(512)(128)(4,1)S(1)} %get-tuple-element.33, bf16[1,1,512,2,128]{4,3,2,1,0:T(2,128)(2,1)S(1)} %copy-done.8), kind=kOutput, calls=%fused_computation.33 | convolution fusion | flops 817827840 | bytes 15954336 | tf_op jit(solution)/shard_map/qhgk,khd->hgqd/dot_general | solution.py:24
  125.2 16.5 %pmax.7 = f32[1024,2,6]{0,2,1:T(8,128)S(1)} all-reduce(f32[1024,2,6]{0,2,1:T(8,128)S(1)} %get-tuple-element.6), channel_id=1, replica_groups=mesh['rep'=16,'wide'=4,'narrow'=4] {'narrow'}, use_global_device_ids=true, to_apply=%region_5.6 | all-reduce | flops 12288 | bytes 98304 | tf_op jit(solution)/shard_map/pmax | solution.py:124
  141.7 0.1 fusion.69
  141.8 0.1 concatenate.35
  141.9 0.1 concatenate.36
  142.0 0.1 concatenate.37
  142.1 0.2 copy.104
  142.3 0.2 copy.103
  142.5 0.2 copy.102
  142.8 8.7 %fusion.10 = bf16[2,6,1024,128]{3,2,1,0:T(8,128)(2,1)S(1)} fusion(f32[2,6,4,128]{3,2,1,0:T(4,128)S(1)} %bitcast.161, f32[2,6,510,128]{3,2,1,0:T(8,128)} %fusion.25, f32[2,6,510,128]{3,2,1,0:T(8,128)} %fusion.22, f32[2,6,1024]{2,1,0:T(8,128)S(1)} %get-tuple-element.19, f32[2,6,1024]{2,1,0:T(8,128)S(1)} %get-tuple-element.17, ...), kind=kOutput, calls=%fused_computation.17 | convolution fusion | flops 216268800 | bytes 12902400 | tf_op jit(solution)/shard_map/rhgk,khd->hgrd/dot_general | solution.py:24
  151.4 3.3 %maximum_maximum_fusion = bf16[13,4,4,64,128]{4,3,1,2,0:T(8,128)(2,1)} fusion(bf16[1,4,4,64,12]{4,3,1,2,0:T(8,128)(2,1)S(1)} %copy.104, bf16[1,4,4,64,12]{4,3,1,2,0:T(8,128)(2,1)S(1)} %copy.103, bf16[1,4,4,64,12]{4,3,1,2,0:T(8,128)(2,1)S(1)} %copy.102, bf16[13,128]{1,0:T(8,128)(2,1)S(1)} %pad.4.clone, bf16[12,4,4,64,128]{4,3,2,1,0:T(8,128)(2,1)S(1)} %bitcast.158), kind=kLoop, calls=%fused_computation.25 | loop fusion | flops 17039360 | bytes 6630656 | tf_op jit(solution)/shard_map/concatenate | solution.py:145
  154.7 0.0 reduce-scatter.2.cloned.1.call-update
  154.7 41.7 %reduce-scatter.2.cloned.1.call-done = bf16[13,256,128]{2,1,0:T(8,128)(2,1)} async-done(((bf16[13,1024,128]{2,1,0:T(8,128)(2,1)}), bf16[13,256,128]{2,1,0:T(8,128)(2,1)}) %reduce-scatter.2.cloned.1.call-update) | async-done | bytes 851984 | tf_op jit(solution)/shard_map/reduce_scatter | solution.py:152
  196.4 1.2 copy.106
  197.7 17.0 %all_to_all.10 = bf16[13,4,64,128]{3,2,0,1:T(8,128)(2,1)S(1)} all-to-all(bf16[13,4,64,128]{3,2,0,1:T(8,128)(2,1)S(1)} %copy.106), channel_id=1, replica_groups=mesh['rep'=16,'wide'=4,'narrow'=4] {'wide'}, dimensions={1} | all-to-all | bytes 1703936 | tf_op jit(solution)/shard_map/all_to_all | solution.py:153
  214.6 0.2 convert_element_type.44
  214.8 0.1 fusion.89
  215.0 0.1 fusion.52
  215.1 0.1 copy.107
  215.2 0.5 fusion.32
  215.7 0.1 copy.109
  215.8 0.2 copy_bitcast_fusion.12
  216.0 13.5 %all_gather.23 = bf16[256,1536]{1,0:T(8,128)(2,1)S(1)} all-gather(bf16[64,1536]{1,0:T(8,128)(2,1)S(1)} %copy_bitcast_fusion.12), channel_id=1, replica_groups=mesh['rep'=16,'wide'=4,'narrow'=4] {'narrow'}, dimensions={0}, use_global_device_ids=true | all-gather | bytes 983040 | tf_op jit(solution)/shard_map/all_gather | solution.py:162
  229.5 1.3 fusion.42
  (33 shorter events, 0.1 us)
Async XLA Ops:
  6.5 222.9 %copy-start = (bf16[1536,384]{1,0:T(8,128)(2,1)S(1)}, bf16[1536,384]{1,0:T(8,128)(2,1)}, u32[]{:S(2)}) copy-start(bf16[1536,384]{1,0:T(8,128)(2,1)} %param.11) | copy-start | bytes 3538948
  6.5 37.7 %copy-start.12 = (s32[2]{0:T(128)S(1)}, s32[2]{0:T(128)}, u32[]{:S(2)}) copy-start(s32[2]{0:T(128)} %param.14) | copy-start | bytes 28
  6.5 37.9 %copy-start.13 = (s32[4]{0:T(128)S(1)}, s32[4]{0:T(128)}, u32[]{:S(2)}) copy-start(s32[4]{0:T(128)} %param.15) | copy-start | bytes 52
  6.5 40.9 %copy-start.6 = (bf16[2,2,512,2,128]{4,3,2,1,0:T(2,128)(2,1)S(1)}, bf16[2,2,512,2,128]{4,3,2,1,0:T(2,128)(2,1)}, u32[]{:S(2)}) copy-start(bf16[2,2,512,2,128]{4,3,2,1,0:T(2,128)(2,1)} %param.12) | copy-start | bytes 3145732
  6.5 34.2 %all-gather.5.cloned.1.call-start = ((), (), s32[]{:S(2)}) async-start(), calls=%async_computation.4 | async-start | bytes 1966080 | tf_op jit(solution)/shard_map/all_gather | solution.py:70
  7.3 90.0 %all-gather.7.cloned.1.call-start = ((), (), s32[]{:S(2)}) async-start(), calls=%async_computation.5 | async-start | bytes 3342336 | tf_op jit(solution)/shard_map/all_gather | solution.py:76
  42.8 0.7 copy-start.7
  44.4 4.6 %copy-start.4 = (bf16[2,4,512,2,128]{4,3,2,1,0:T(2,128)(2,1)S(1)}, bf16[2,4,512,2,128]{4,3,2,1,0:T(2,128)(2,1)}, u32[]{:S(2)}) copy-start(bf16[2,4,512,2,128]{4,3,2,1,0:T(2,128)(2,1)} %param.13) | copy-start | bytes 6291460
  52.0 58.4 %all-to-all-start = ((bf16[4,64,128]{2,1,0:T(8,128)(2,1)}), bf16[4,64,128]{2,1,0:T(8,128)(2,1)}, u32[]{:S(2)}, u32[]{:S(2)}) async-start(bf16[4,64,128]{2,1,0:T(8,128)(2,1)} %bitcast.160), calls=%async_computation | async-start | bytes 131072 | tf_op jit(solution)/shard_map/all_to_all | solution.py:83
  56.3 140.2 %reduce-scatter.2.cloned.1.call-start = ((), (), s32[]{:S(2)}) async-start(), calls=%async_computation.3 | async-start | bytes 4259840 | tf_op jit(solution)/shard_map/reduce_scatter | solution.py:152
  97.3 3.1 %copy-start.10 = (bf16[1,1,512,2,128]{4,3,2,1,0:T(2,128)(2,1)S(1)}, bf16[1,1,512,2,128]{4,3,2,1,0:T(2,128)(2,1)}, u32[]{:S(2)}) copy-start(bf16[1,1,512,2,128]{4,3,2,1,0:T(2,128)(2,1)} %get-tuple-element.10) | copy-start | bytes 786436
  99.6 2.7 %copy-start.1 = (bf16[4,256,3,4,128]{4,1,0,3,2:T(8,128)(2,1)}, bf16[4,256,3,4,128]{4,1,0,3,2:T(8,128)(2,1)S(1)}, u32[]{:S(2)}) copy-start(bf16[4,256,3,4,128]{4,1,0,3,2:T(8,128)(2,1)S(1)} %copy.85) | copy-start | bytes 9437188
  102.3 3.6 %copy-start.9 = (bf16[1,1,512,2,128]{4,3,2,1,0:T(2,128)(2,1)S(1)}, bf16[1,1,512,2,128]{4,3,2,1,0:T(2,128)(2,1)}, u32[]{:S(2)}) copy-start(bf16[1,1,512,2,128]{4,3,2,1,0:T(2,128)(2,1)} %get-tuple-element.12) | copy-start | bytes 786436
  105.9 4.5 %copy-start.5 = (pred[1024,64]{0,1:T(8,128)(4,1)S(1)}, pred[1024,64]{0,1:T(8,128)(4,1)}, u32[]{:S(2)}) copy-start(pred[1024,64]{0,1:T(8,128)(4,1)} %compare_and_fusion) | copy-start | bytes 196612
  110.4 5.0 %copy-start.2 = (bf16[4,256,3,4,128]{4,1,0,3,2:T(8,128)(2,1)S(1)}, bf16[4,256,3,4,128]{4,1,0,3,2:T(8,128)(2,1)}, u32[]{:S(2)}) copy-start(bf16[4,256,3,4,128]{4,1,0,3,2:T(8,128)(2,1)} %copy-done.1) | copy-start | bytes 9437188
  113.7 1.7 copy-start.3
  117.4 3.6 %copy-start.8 = (bf16[1,1,512,2,128]{4,3,2,1,0:T(2,128)(2,1)S(1)}, bf16[1,1,512,2,128]{4,3,2,1,0:T(2,128)(2,1)}, u32[]{:S(2)}) copy-start(bf16[1,1,512,2,128]{4,3,2,1,0:T(2,128)(2,1)} %get-tuple-element.9) | copy-start | bytes 786436
  214.6 14.8 %copy-start.11 = (bf16[256,384]{1,0:T(8,128)(2,1)S(1)}, bf16[256,384]{1,0:T(8,128)(2,1)}, u32[]{:S(2)}) copy-start(bf16[256,384]{1,0:T(8,128)(2,1)} %param.8) | copy-start | bytes 589828
Sparse Core Ops, SparseCore 0:
  9.2 31.5 all-gather.4
  44.4 52.8 all-gather.6
  154.8 41.5 reduce-scatter.1
where the time goes:
time: 238 us; the launch traced here: 237 us
  waiting for transfers between devices  102 us (43%)
  blocking collectives  61.7 us (26%)
  matrix products  28.1 us (12%)
  other arithmetic  15.4 us (6%)
  between operations  13.4 us (6%)
  local copies, waits for them, and re-layouts  12.4 us (5%)
  starting transfers between devices  4.37 us (2%)
    reduce_scatter x1, waiting for transfers between devices, per_device(): packed = lax.psum_scatter(packed, 'narrow', scatter_dimension=1, tiled=True)  41.7 us
    all_gather x1, waiting for transfers between devices, per_device(): lax.all_gather(part[:, :q_blocks], ('wide', 'narrow'), axis=0, tiled=False)  41 us
    all_gather x1, waiting for transfers between devices, per_device(): w_cols = lax.all_gather(w_qkv, 'wide', axis=0, tiled=False)  18.4 us
    dot_general x4, matrix products, partial_softmax(): jnp.einsum(form_o, weights.astype(jnp.bfloat16), values, preferred_elemen...  17.4 us
    all_to_all x1, blocking collectives, per_device(): lax.all_to_all(packed.reshape(slots, n_wide, own, head_dim), 'wide', 1, 1)  17 us
    pmax x1, blocking collectives, per_device(): top = lax.pmax(peak, 'narrow')  16.5 us
    all_gather x1, blocking collectives, per_device(): features = lax.all_gather(tokens, 'narrow', axis=1, tiled=True)  14.8 us
    all_gather x1, blocking collectives, per_device(): mine_rows = lax.all_gather(attended, 'narrow', axis=0, tiled=True)  13.5 us
  transfers between devices with their start and end apart: 4, of which 3 were waited for; matrix products, arithmetic and copies ran while one was open for 9% of the time, Pallas kernels for 0%

commit v1 on v0

--- a/solution.py
+++ b/solution.py
@@ -2,6 +2,7 @@
 import jax.numpy as jnp
 from jax import lax
 from jax.sharding import PartitionSpec as P
+from jax.lax import all_to_all, psum
 
 EPS = 1e-06
 NEG = -1e30
@@ -65,7 +66,12 @@
     own_start = joined * own
     own_pos = lax.dynamic_slice_in_dim(positions, own_start, own)
     own_seq = lax.dynamic_slice_in_dim(sequence, own_start, own)
-    features = lax.all_gather(tokens, "narrow", axis=1, tiled=True)
+    n_axis = psum(1, axis_name="narrow")
+    views = []
+    for dev_j in [*range(tokens.ndim)]:
+        views.append(n_axis if dev_j == 1 else 1)
+    plain = jnp.tile(tokens, views)
+    features = all_to_all(plain, "narrow", split_axis=1, concat_axis=1, tiled=True)
     normed_rows = normalize(features, attn_gain)
     w_cols = lax.all_gather(w_qkv, "wide", axis=0, tiled=False)
     part = jnp.einsum(

time: 238 us -> 238 us (level)
  waiting for transfers between devices: 102 us -> 96.8 us
  local copies, waits for them, and re-layouts: 12.4 us -> 14.9 us
    all_to_all x0 -> x1, blocking collectives: none -> 16.6 us  [per_device(): all_to_all(plain, 'narrow', split_axis=1, concat_axis=1, tiled=True)]
    all_gather x1 -> x0, blocking collectives: 14.8 us -> none  [per_device(): features = lax.all_gather(tokens, 'narrow', axis=1, tiled=True)]
    all_gather x1, waiting for transfers between devices: 18.4 us -> 14.2 us  [per_device(): w_cols = lax.all_gather(w_qkv, 'wide', axis=0, tiled=False)]
  transfers between devices with their start and end apart: 4 -> 4, of which waited for: 3 -> 3; matrix products, arithmetic and copies ran while one was open for 9% -> 10% of each run, Pallas kernels for 0% -> 0%
where the time goes in v1:
time: 238 us
  waiting for transfers between devices  96.8 us (41%)
  blocking collectives  63.5 us (27%)
  matrix products  28.3 us (12%)
  other arithmetic  16.6 us (7%)
  local copies, waits for them, and re-layouts  14.9 us (6%)
  between operations  13.4 us (6%)
  starting transfers between devices  4.32 us (2%)
    reduce_scatter x1, waiting for transfers between devices, per_device(): packed = lax.psum_scatter(packed, 'narrow', scatter_dimension=1, tiled=True)  41.7 us
    all_gather x1, waiting for transfers between devices, per_device(): lax.all_gather(part[:, :q_blocks], ('wide', 'narrow'), axis=0, tiled=False)  40.1 us
    dot_general x4, matrix products, partial_softmax(): jnp.einsum(form_o, weights.astype(jnp.bfloat16), values, preferred_elemen...  17.4 us
    all_to_all x1, blocking collectives, per_device(): lax.all_to_all(packed.reshape(slots, n_wide, own, head_dim), 'wide', 1, 1)  17 us
    all_to_all x1, blocking collectives, per_device(): all_to_all(plain, 'narrow', split_axis=1, concat_axis=1, tiled=True)  16.6 us
    pmax x1, blocking collectives, per_device(): top = lax.pmax(peak, 'narrow')  16.5 us
    all_gather x1, waiting for transfers between devices, per_device(): w_cols = lax.all_gather(w_qkv, 'wide', axis=0, tiled=False)  14.2 us
    all_gather x1, blocking collectives, per_device(): mine_rows = lax.all_gather(attended, 'narrow', axis=0, tiled=True)  13.5 us
  transfers between devices with their start and end apart: 4, of which 3 were waited for; matrix products, arithmetic and copies ran while one was open for 10% of the time, Pallas kernels for 0%

profile of v1, /device:TPU:32, one launch (start us, length us, event | category | flops | bytes accessed | tf_op | source)
XLA Modules:
  0.0 237.8 jit_solution(764749093044653207)
XLA Ops:
  6.5 0.7 all-gather.5.cloned.1.call-update
  7.3 0.0 all-gather.7.cloned.1.call-start
  7.3 1.0 tile.2
  8.3 16.6 %all_to_all.16 = bf16[256,4,384]{2,0,1:T(8,128)(2,1)S(1)} all-to-all(bf16[256,4,384]{2,0,1:T(8,128)(2,1)S(1)} %tile.2), channel_id=1, replica_groups=mesh['rep'=16,'wide'=4,'narrow'=4] {'narrow'}, dimensions={1} | all-to-all | bytes 1572864 | tf_op jit(solution)/shard_map/all_to_all | solution.py:74
  24.9 0.3 copy.110
  25.2 0.2 multiply_reduce_fusion
  25.4 1.2 fusion.35
  26.6 14.2 %all-gather.5.cloned.1.call-done = bf16[6144,128]{1,0:T(8,128)(2,1)} async-done(((bf16[1536,128]{1,0:T(8,128)(2,1)}), bf16[6144,128]{1,0:T(8,128)(2,1)}) %all-gather.5.cloned.1.call-update) | async-done | bytes 1572880 | tf_op jit(solution)/shard_map/all_gather | solution.py:76
  40.8 2.2 convolution_convert_fusion
  43.0 0.7 copy-done.6
  43.7 0.7 slice.80
  44.5 0.1 iota_add_fusion.1
  44.5 0.1 add.103
  44.6 0.1 fusion.67
  44.7 0.1 dynamic_slice.6
  44.8 0.1 dynamic_slice.7
  44.9 0.1 pad.4.clone
  44.9 0.7 fusion.89
  45.6 1.3 fusion.72
  46.9 0.1 broadcast_compare_fusion
  46.9 0.7 compare_and_fusion
  47.7 1.5 fusion.88
  49.2 2.7 %fusion.87 = (bf16[1,4,512,2,128]{4,3,2,1,0:T(2,128)(2,1)S(1)}, bf16[1,4,512,2,128]{4,3,2,1,0:T(2,128)(2,1)S(1)}) fusion(bf16[2,4,512,2,128]{4,3,2,1,0:T(2,128)(2,1)} %param.13), kind=kLoop, calls=%fused_computation.131 | loop fusion | bytes 4194304 | tf_op jit(solution)/shard_map/slice | solution.py:114
  51.9 1.5 slice.84
  53.4 4.3 %all-to-all-start.1 = ((bf16[4,64,128]{2,1,0:T(8,128)(2,1)}), bf16[4,64,128]{2,1,0:T(8,128)(2,1)}, u32[]{:S(2)}, u32[]{:S(2)}) async-start(bf16[4,64,128]{2,1,0:T(8,128)(2,1)} %bitcast.166), calls=%async_computation.1 | async-start | bytes 131072 | tf_op jit(solution)/shard_map/all_to_all | solution.py:89
  57.7 40.1 %all-gather.7.cloned.1.call-done = bf16[4096,3,128]{2,0,1:T(8,128)(2,1)} async-done(((bf16[256,3,128]{2,0,1:T(8,128)(2,1)}), bf16[4096,3,128]{2,0,1:T(8,128)(2,1)}) %all-gather.7.cloned.1.call-update) | async-done | bytes 3145744 | tf_op jit(solution)/shard_map/all_gather | solution.py:82
  97.8 2.3 copy.112
  100.1 0.4 fusion.43
  100.5 0.2 fusion.84
  100.6 0.2 fusion.62
  100.8 1.9 bitcast_reduce_fusion
  102.8 3.6 %fusion.6 = f32[510,2,6]{0,2,1:T(8,128)S(1)} fusion(f32[2,510,6,512]{3,1,2,0:T(8,128)S(1)} %get-tuple-element.27, f32[510,2,6]{0,2,1:T(8,128)S(1)} %get-tuple-element.26, pred[512]{0:T(512)(128)(4,1)S(1)} %get-tuple-element.32), kind=kLoop, calls=%fused_computation.12 | loop fusion | flops 15661080 | bytes 12583232 | tf_op jit(solution)/shard_map/reduce_sum | solution.py:24
  106.3 4.2 %fusion.25 = f32[2,6,510,128]{3,2,1,0:T(8,128)} fusion(f32[2,510,6,512]{3,1,2,0:T(8,128)S(1)} %get-tuple-element.27, f32[510,2,6]{0,2,1:T(8,128)S(1)} %get-tuple-element.26, pred[512]{0:T(512)(128)(4,1)S(1)} %get-tuple-element.32, bf16[1,1,512,2,128]{4,3,2,1,0:T(2,128)(2,1)S(1)} %copy-done.8), kind=kOutput, calls=%fused_computation.32 | convolution fusion | flops 817827840 | bytes 15954336 | tf_op jit(solution)/shard_map/qhgk,khd->hgqd/dot_general | solution.py:25
  110.6 0.2 fusion.42
  110.9 3.3 %fusion.19 = (f32[1024,2,6]{0,2,1:T(8,128)S(1)}, f32[2,64,1024,6]{2,1,3,0:T(8,128)S(1)}) fusion(pred[1024,64]{0,1:T(8,128)(4,1)S(1)} %copy-done.4, bf16[1024,2,6,128]{3,0,2,1:T(8,128)(2,1)} %bitcast.160, bf16[4,64,128]{2,1,0:T(8,128)(2,1)} %all-to-all-done.1), kind=kOutput, calls=%fused_computation.28 | convolution fusion | flops 203673600 | bytes 6438912 | tf_op jit(solution)/shard_map/rhgd,khd->rhgk/dot_general | solution.py:18
  114.2 0.8 fusion.20
  115.0 0.8 copy-done.3
  115.9 1.9 bitcast_reduce_fusion.1
  117.8 0.1 fusion.74
  117.9 3.6 %fusion.4 = f32[510,2,6]{0,2,1:T(8,128)S(1)} fusion(f32[2,510,6,512]{3,1,2,0:T(8,128)S(1)} %get-tuple-element.29, f32[510,2,6]{0,2,1:T(8,128)S(1)} %get-tuple-element.28, pred[512]{0:T(512)(128)(4,1)S(1)} %get-tuple-element.33), kind=kLoop, calls=%fused_computation.10 | loop fusion | flops 15661080 | bytes 12583232 | tf_op jit(solution)/shard_map/reduce_sum | solution.py:24
  121.4 4.3 %fusion.22 = f32[2,6,510,128]{3,2,1,0:T(8,128)} fusion(f32[2,510,6,512]{3,1,2,0:T(8,128)S(1)} %get-tuple-element.29, f32[510,2,6]{0,2,1:T(8,128)S(1)} %get-tuple-element.28, pred[512]{0:T(512)(128)(4,1)S(1)} %get-tuple-element.33, bf16[1,1,512,2,128]{4,3,2,1,0:T(2,128)(2,1)S(1)} %copy-done.7), kind=kOutput, calls=%fused_computation.31 | convolution fusion | flops 817827840 | bytes 15954336 | tf_op jit(solution)/shard_map/qhgk,khd->hgqd/dot_general | solution.py:25
  125.7 16.5 %pmax.7 = f32[1024,2,6]{0,2,1:T(8,128)S(1)} all-reduce(f32[1024,2,6]{0,2,1:T(8,128)S(1)} %get-tuple-element.6), channel_id=1, replica_groups=mesh['rep'=16,'wide'=4,'narrow'=4] {'narrow'}, use_global_device_ids=true, to_apply=%region_5.6 | all-reduce | flops 12288 | bytes 98304 | tf_op jit(solution)/shard_map/pmax | solution.py:130
  142.2 0.1 fusion.65
  142.3 0.1 concatenate.35
  142.4 0.1 concatenate.36
  142.5 0.1 concatenate.37
  142.6 0.2 copy.131
  142.8 0.2 copy.130
  143.0 0.2 copy.129
  143.3 8.7 %fusion.10 = bf16[2,6,1024,128]{3,2,1,0:T(8,128)(2,1)S(1)} fusion(f32[2,6,4,128]{3,2,1,0:T(4,128)S(1)} %bitcast.167, f32[2,6,510,128]{3,2,1,0:T(8,128)} %fusion.25, f32[2,6,510,128]{3,2,1,0:T(8,128)} %fusion.22, f32[2,6,1024]{2,1,0:T(8,128)S(1)} %get-tuple-element.19, f32[2,6,1024]{2,1,0:T(8,128)S(1)} %get-tuple-element.17, ...), kind=kOutput, calls=%fused_computation.17 | convolution fusion | flops 216268800 | bytes 12902400 | tf_op jit(solution)/shard_map/rhgk,khd->hgrd/dot_general | solution.py:25
  151.9 3.3 %maximum_maximum_fusion = bf16[13,4,4,64,128]{4,3,1,2,0:T(8,128)(2,1)} fusion(bf16[1,4,4,64,12]{4,3,1,2,0:T(8,128)(2,1)S(1)} %copy.131, bf16[1,4,4,64,12]{4,3,1,2,0:T(8,128)(2,1)S(1)} %copy.130, bf16[1,4,4,64,12]{4,3,1,2,0:T(8,128)(2,1)S(1)} %copy.129, bf16[13,128]{1,0:T(8,128)(2,1)S(1)} %pad.4.clone, bf16[12,4,4,64,128]{4,3,2,1,0:T(8,128)(2,1)S(1)} %bitcast.164), kind=kLoop, calls=%fused_computation.25 | loop fusion | flops 17039360 | bytes 6630656 | tf_op jit(solution)/shard_map/concatenate | solution.py:151
  155.2 0.0 reduce-scatter.2.cloned.1.call-update
  155.2 41.7 %reduce-scatter.2.cloned.1.call-done = bf16[13,256,128]{2,1,0:T(8,128)(2,1)} async-done(((bf16[13,1024,128]{2,1,0:T(8,128)(2,1)}), bf16[13,256,128]{2,1,0:T(8,128)(2,1)}) %reduce-scatter.2.cloned.1.call-update) | async-done | bytes 851984 | tf_op jit(solution)/shard_map/reduce_scatter | solution.py:158
  196.9 1.2 copy.133
  198.2 17.0 %all_to_all.17 = bf16[13,4,64,128]{3,2,0,1:T(8,128)(2,1)S(1)} all-to-all(bf16[13,4,64,128]{3,2,0,1:T(8,128)(2,1)S(1)} %copy.133), channel_id=1, replica_groups=mesh['rep'=16,'wide'=4,'narrow'=4] {'wide'}, dimensions={1} | all-to-all | bytes 1703936 | tf_op jit(solution)/shard_map/all_to_all | solution.py:159
  215.1 0.2 convert_element_type.52
  215.3 0.1 fusion.85
  215.5 0.1 fusion.48
  215.6 0.1 copy.134
  215.7 0.5 fusion.29
  216.2 0.1 copy.136
  216.3 0.2 copy_bitcast_fusion.12
  216.5 13.5 %all_gather.19 = bf16[256,1536]{1,0:T(8,128)(2,1)S(1)} all-gather(bf16[64,1536]{1,0:T(8,128)(2,1)S(1)} %copy_bitcast_fusion.12), channel_id=1, replica_groups=mesh['rep'=16,'wide'=4,'narrow'=4] {'narrow'}, dimensions={0}, use_global_device_ids=true | all-gather | bytes 983040 | tf_op jit(solution)/shard_map/all_gather | solution.py:168
  230.0 1.3 fusion.41
  (36 shorter events, 0.1 us)
Async XLA Ops:
  6.5 223.5 %copy-start = (bf16[1536,384]{1,0:T(8,128)(2,1)S(1)}, bf16[1536,384]{1,0:T(8,128)(2,1)}, u32[]{:S(2)}) copy-start(bf16[1536,384]{1,0:T(8,128)(2,1)} %param.11) | copy-start | bytes 3538948
  6.5 18.9 %copy-start.11 = (f32[1536]{0:T(1024)S(1)}, f32[1536]{0:T(1024)}, u32[]{:S(2)}) copy-start(f32[1536]{0:T(1024)} %param.9) | copy-start | bytes 18436
  6.5 34.2 %all-gather.5.cloned.1.call-start = ((), (), s32[]{:S(2)}) async-start(), calls=%async_computation.5 | async-start | bytes 1966080 | tf_op jit(solution)/shard_map/all_gather | solution.py:76
  7.3 90.5 %all-gather.7.cloned.1.call-start = ((), (), s32[]{:S(2)}) async-start(), calls=%async_computation.6 | async-start | bytes 3342336 | tf_op jit(solution)/shard_map/all_gather | solution.py:82
  25.1 19.3 %copy-start.12 = (s32[2]{0:T(128)S(1)}, s32[2]{0:T(128)}, u32[]{:S(2)}) copy-start(s32[2]{0:T(128)} %param.14) | copy-start | bytes 28
  25.2 19.5 %copy-start.13 = (s32[4]{0:T(128)S(1)}, s32[4]{0:T(128)}, u32[]{:S(2)}) copy-start(s32[4]{0:T(128)} %param.15) | copy-start | bytes 52
  25.2 22.5 %copy-start.5 = (bf16[2,2,512,2,128]{4,3,2,1,0:T(2,128)(2,1)S(1)}, bf16[2,2,512,2,128]{4,3,2,1,0:T(2,128)(2,1)}, u32[]{:S(2)}) copy-start(bf16[2,2,512,2,128]{4,3,2,1,0:T(2,128)(2,1)} %param.12) | copy-start | bytes 3145732
  43.0 0.7 copy-start.6
  53.4 57.5 %all-to-all-start.1 = ((bf16[4,64,128]{2,1,0:T(8,128)(2,1)}), bf16[4,64,128]{2,1,0:T(8,128)(2,1)}, u32[]{:S(2)}, u32[]{:S(2)}) async-start(bf16[4,64,128]{2,1,0:T(8,128)(2,1)} %bitcast.166), calls=%async_computation.1 | async-start | bytes 131072 | tf_op jit(solution)/shard_map/all_to_all | solution.py:89
  57.7 139.3 %reduce-scatter.2.cloned.1.call-start = ((), (), s32[]{:S(2)}) async-start(), calls=%async_computation.4 | async-start | bytes 4259840 | tf_op jit(solution)/shard_map/reduce_scatter | solution.py:158
  97.8 3.1 %copy-start.9 = (bf16[1,1,512,2,128]{4,3,2,1,0:T(2,128)(2,1)S(1)}, bf16[1,1,512,2,128]{4,3,2,1,0:T(2,128)(2,1)}, u32[]{:S(2)}) copy-start(bf16[1,1,512,2,128]{4,3,2,1,0:T(2,128)(2,1)} %get-tuple-element.10) | copy-start | bytes 786436
  100.1 2.7 %copy-start.1 = (bf16[4,256,3,4,128]{4,1,0,3,2:T(8,128)(2,1)}, bf16[4,256,3,4,128]{4,1,0,3,2:T(8,128)(2,1)S(1)}, u32[]{:S(2)}) copy-start(bf16[4,256,3,4,128]{4,1,0,3,2:T(8,128)(2,1)S(1)} %copy.112) | copy-start | bytes 9437188
  102.7 3.6 %copy-start.8 = (bf16[1,1,512,2,128]{4,3,2,1,0:T(2,128)(2,1)S(1)}, bf16[1,1,512,2,128]{4,3,2,1,0:T(2,128)(2,1)}, u32[]{:S(2)}) copy-start(bf16[1,1,512,2,128]{4,3,2,1,0:T(2,128)(2,1)} %get-tuple-element.12) | copy-start | bytes 786436
  106.3 4.5 %copy-start.4 = (pred[1024,64]{0,1:T(8,128)(4,1)S(1)}, pred[1024,64]{0,1:T(8,128)(4,1)}, u32[]{:S(2)}) copy-start(pred[1024,64]{0,1:T(8,128)(4,1)} %compare_and_fusion) | copy-start | bytes 196612
  110.9 5.0 %copy-start.2 = (bf16[4,256,3,4,128]{4,1,0,3,2:T(8,128)(2,1)S(1)}, bf16[4,256,3,4,128]{4,1,0,3,2:T(8,128)(2,1)}, u32[]{:S(2)}) copy-start(bf16[4,256,3,4,128]{4,1,0,3,2:T(8,128)(2,1)} %copy-done.1) | copy-start | bytes 9437188
  114.2 1.7 copy-start.3
  117.9 3.6 %copy-start.7 = (bf16[1,1,512,2,128]{4,3,2,1,0:T(2,128)(2,1)S(1)}, bf16[1,1,512,2,128]{4,3,2,1,0:T(2,128)(2,1)}, u32[]{:S(2)}) copy-start(bf16[1,1,512,2,128]{4,3,2,1,0:T(2,128)(2,1)} %get-tuple-element.9) | copy-start | bytes 786436
  215.1 14.9 %copy-start.10 = (bf16[256,384]{1,0:T(8,128)(2,1)S(1)}, bf16[256,384]{1,0:T(8,128)(2,1)}, u32[]{:S(2)}) copy-start(bf16[256,384]{1,0:T(8,128)(2,1)} %param.8) | copy-start | bytes 589828
Sparse Core Ops, SparseCore 0:
  9.1 31.5 all-gather.4
  44.6 53.1 all-gather.6
  155.3 41.5 reduce-scatter.1
